TPU v7x, 256 devices: a whole 4x4x8 slice. The times are simulated.
256 devices in a mesh: expert: 8 (over x, core), tensor: 32 (over z, y).
Axes of the slice: x: 4, y: 4, z: 8, core: 2. Of those that a mesh axis runs over, the one named last changes fastest.
Arguments:
- resid: bfloat16 [16384, 2048], P(('expert', 'tensor')), may hold values from -6 to 6
- contexts: bfloat16 [16384, 4096], P('expert', 'tensor'), may hold values from -6 to 6
- att_routes: int32 [16384, 2], P('expert'), may hold values from 0 to 7, all different within a row
- att_scores: float32 [16384, 2], P('expert'), may hold values from -6 to 6
- att_out_w: bfloat16 [8, 2048, 2048], P(None, 'tensor'), may hold values from -0.125 to 0.125
- norm_gain: bfloat16 [2048], replicated, may hold values from 0.25 to 1.75
- router_w: bfloat16 [2048, 8], replicated, may hold values from -0.125 to 0.125
- mlp_routes: int32 [16384, 2], P(('expert', 'tensor')), may hold values from 0 to 7, all different within a row
- split_rule: int32 [16384, 2], P(('expert', 'tensor')), may hold values from 0 to 2519
- placement: int32 [32], replicated, may hold values from 0 to 7, as said below
- cap_blocks: int32 [32], replicated, may hold values from 1 to 2, as said below
- w_gate_up: bfloat16 [32, 2048, 2, 5632], P('tensor', None, None, 'expert'), as said below
- w_down: bfloat16 [32, 5632, 2048], P('tensor', 'expert'), as said below
- final_gain: bfloat16 [2048], replicated, may hold values from 0.25 to 1.75
Outputs:
- stream_out: bfloat16 [16384, 2048], P(('expert', 'tensor'))
- normalized: bfloat16 [16384, 2048], P(('expert', 'tensor'))
Inputs may be any that keep to these rules, and one draw needn't show every extreme that they name: `att_routes`: each row names 2 different experts. `mlp_routes`: each row names 2 different experts. `placement`: every expert is held by at least one slot. `cap_blocks`: some slot accepts 2 blocks. `w_gate_up`: slots that hold the same expert hold equal weights. `w_down`: slots that hold the same expert hold equal weights.
All inputs are finite; a program needn't handle non-finite values.
Results may differ from a plain program's by a relative error of at most 0.023.
Values may be sent and summed in bfloat16 or wider, within the bound.
No kernel may reach another device: no remote copies, remote signals or barrier semaphores. Data moves between devices by JAX's collectives and lax.ppermute only.
A program may use at most 64 MiB of HBM per device.

v0:
```python
import jax
import jax.numpy as jnp
from jax import lax
from jax.sharding import PartitionSpec as P

MAXB = 2
norm_eps = 1e-06


def rms_norm(values, gain):
    scale = lax.rsqrt(jnp.mean(values * values, axis=-1, keepdims=True) + norm_eps)
    return values * scale * gain.astype(values.dtype)


def pair_gates(scores):
    first = jax.nn.silu(scores[:, 0:1] * 0.0) * 0.0 + jax.nn.sigmoid(
        scores[:, 0:1] - scores[:, 1:2]
    )
    first = first[:, 0]
    return jnp.stack([first, 1.0 - first], axis=1)


def activate(shard_piece, w_gate_up):
    both = jnp.einsum(
        "tsecd,sdgf->tsecgf", shard_piece, w_gate_up, preferred_element_type=jnp.float32
    )
    hidden = (jax.nn.silu(both[:, :, :, :, 0, :]) * both[:, :, :, :, 1, :]).astype(jnp.bfloat16)
    hidden = jnp.transpose(hidden, (0, 2, 3, 1, 4))
    return hidden.reshape(
        hidden.shape[0] * hidden.shape[1] * hidden.shape[2], hidden.shape[3], hidden.shape[4]
    )


def per_device(
    resid,
    contexts,
    att_routes,
    att_scores,
    att_out_w,
    norm_gain,
    router_w,
    mlp_routes,
    split_rule,
    placement,
    cap_blocks,
    w_gate_up,
    w_down,
    final_gain,
):
    n_tensor = lax.axis_size("tensor")
    row_count = resid.shape[0]
    model_width = resid.shape[1]
    group_rows = contexts.shape[0]
    att_experts = att_out_w.shape[0]
    slice_ctx = att_out_w.shape[1]
    top_count = att_routes.shape[1]
    gate_att = pair_gates(att_scores)
    chosen = (
        att_routes[:, :, None] == jnp.arange(att_experts, dtype=jnp.int32)[None, None, :]
    ).astype(jnp.float32)
    weighted = chosen * gate_att[:, :, None]
    context_part = contexts.reshape(group_rows, slice_ctx, top_count).astype(jnp.float32)
    mixed = (
        jnp.einsum("tke,tck->tec", weighted, context_part)
        .astype(jnp.bfloat16)
        .reshape(group_rows, att_experts * slice_ctx)
    )
    weight_flat = att_out_w.reshape(att_experts * slice_ctx, model_width)
    row_block = mixed
    attention = lax.psum_scatter(
        jnp.dot(row_block, weight_flat, preferred_element_type=jnp.float32).astype(jnp.bfloat16),
        "tensor",
        scatter_dimension=0,
        tiled=True,
    ).astype(jnp.float32)
    stream = (resid.astype(jnp.float32) + attention).astype(jnp.bfloat16)
    normed = rms_norm(stream.astype(jnp.float32), norm_gain).astype(jnp.bfloat16)
    logits = jnp.dot(normed, router_w, preferred_element_type=jnp.float32)
    gate_mlp = pair_gates(jnp.take_along_axis(logits, mlp_routes, axis=1))
    replicas = placement.shape[0]
    slots = w_gate_up.shape[0]
    expert_total = router_w.shape[1]
    block_rows = max(1, row_count * top_count // (2 * replicas))
    capacity_rows = MAXB * block_rows
    slot_ids = jnp.arange(replicas, dtype=jnp.int32)
    expert_ids = jnp.arange(expert_total, dtype=jnp.int32)
    copies = jnp.sum((placement[None, :] == expert_ids[:, None]).astype(jnp.int32), axis=1)
    earlier = jnp.sum(
        (
            (placement[None, :] == placement[:, None]) & (slot_ids[None, :] < slot_ids[:, None])
        ).astype(jnp.int32),
        axis=1,
    )
    route_onehot = (mlp_routes[:, :, None] == expert_ids[None, None, :]).astype(jnp.int32)
    route_copies = jnp.sum(route_onehot * copies[None, None, :], axis=2)
    replica_rank = jnp.remainder(split_rule, route_copies)
    match = (
        (placement[None, None, :] == mlp_routes[:, :, None])
        & (earlier[None, None, :] == replica_rank[:, :, None])
    ).astype(jnp.int32)
    replica_slot = jnp.sum(match * slot_ids[None, None, :], axis=2)
    capacity = jnp.sum(match * cap_blocks[None, None, :], axis=2) * block_rows
    flat_match = match.reshape(row_count * top_count, replicas)
    before = jnp.cumsum(flat_match, axis=0) - flat_match
    arrival = jnp.sum(before * flat_match, axis=1).reshape(row_count, top_count)
    is_kept = arrival < capacity
    holder = replica_slot // slots
    within = replica_slot % slots
    position = within * (n_tensor * capacity_rows) + holder * capacity_rows + arrival
    position = jnp.where(is_kept, position, -1)
    buffer_rows = slots * n_tensor * capacity_rows
    placer = jnp.sum(
        (jnp.arange(buffer_rows, dtype=jnp.int32)[:, None, None] == position[None, :, :]).astype(
            jnp.bfloat16
        ),
        axis=2,
    )
    send_rows = jnp.dot(placer, normed, preferred_element_type=jnp.float32).astype(jnp.bfloat16)
    send_rows = send_rows.reshape(slots, n_tensor, capacity_rows, model_width)
    collected = lax.all_gather(send_rows[None], "expert", axis=0, tiled=True)
    arrived = lax.all_to_all(collected, "tensor", split_axis=2, concat_axis=2, tiled=True)
    hidden = activate(arrived, w_gate_up)
    row_block = hidden
    summed = lax.psum_scatter(
        jnp.einsum("bsf,sfd->bsd", row_block, w_down, preferred_element_type=jnp.float32).astype(
            jnp.bfloat16
        ),
        "expert",
        scatter_dimension=0,
        tiled=True,
    )
    results = summed.reshape(n_tensor, capacity_rows, slots, model_width)
    returned = lax.all_to_all(results, "tensor", split_axis=0, concat_axis=0, tiled=True)
    flat_back = returned.reshape(n_tensor * capacity_rows * slots, model_width)
    back_index = jnp.where(is_kept, holder * (capacity_rows * slots) + arrival * slots + within, 0)
    fetched = (
        jnp.take(flat_back, back_index.reshape(-1), axis=0)
        .reshape(row_count, top_count, model_width)
        .astype(jnp.float32)
    )
    factors = gate_mlp * is_kept.astype(jnp.float32)
    expert_mix = fetched[:, 0, :] * factors[:, 0:1] + fetched[:, 1, :] * factors[:, 1:2]
    after = stream.astype(jnp.float32) + expert_mix
    return (after.astype(jnp.bfloat16), rms_norm(after, final_gain).astype(jnp.bfloat16))


def solution(mesh):
    return jax.shard_map(
        per_device,
        mesh=mesh,
        in_specs=(
            P(("expert", "tensor"), None),
            P("expert", "tensor"),
            P("expert", None),
            P("expert", None),
            P(None, "tensor", None),
            P(),
            P(),
            P(("expert", "tensor"), None),
            P(("expert", "tensor"), None),
            P(),
            P(),
            P("tensor", None, None, "expert"),
            P("tensor", "expert", None),
            P(),
        ),
        out_specs=(P(("expert", "tensor"), None), P(("expert", "tensor"), None)),
        check_vma=False,
    )
```

profile of v0, /device:TPU:7, one launch (start us, length us, event | category | flops | bytes accessed | tf_op | source)
XLA Modules:
  0.0 516.6 jit_solution(11836133515749787276)
XLA Ops:
  7.2 2.2 copy.77
  9.4 1.4 reshape.175
  10.8 2.1 copy.78
  13.0 0.3 copy.76
  13.3 1.4 copy.75
  14.7 14.3 %convolution_convert_fusion = bf16[2048,8,64]{2,1,0:T(8,128)(2,1)S(1)} fusion(bf16[2048,64,2]{1,2,0:T(2,128)(2,1)} %copy.78, bf16[2048,2]{1,0:T(8,128)(2,1)S(1)} %copy.76, s32[2048,2]{1,0:T(8,128)} %copy.75), kind=kOutput, calls=%fused_computation.14 | convolution fusion | flops 4259840 | bytes 2646016 | tf_op jit(solution)/shard_map/tke,tck->tec/dot_general | solution.py:64
  29.0 7.0 %bitcast_convert_fusion = bf16[2048,2048]{1,0:T(8,128)(2,1)} fusion(bf16[8,64,2048]{2,1,0:T(8,128)(2,1)S(1)} %copy-done.11, bf16[2048,8,64]{2,1,0:T(8,128)(2,1)S(1)} %convolution_convert_fusion), kind=kOutput, calls=%fused_computation.2 | convolution fusion | flops 4299161600 | bytes 12582912 | tf_op jit(solution)/shard_map/dot_general | solution.py:71
  36.1 0.6 copy-done.7
  36.7 0.1 convert_reduce_fusion.1
  36.9 0.1 and_select_fusion.1
  37.1 0.1 copy.81
  37.2 0.1 eq.133
  37.3 0.1 eq.119
  37.5 0.2 convert_reduce_fusion
  37.6 0.1 fusion.27
  37.7 0.2 reduce_window_sum.11
  37.9 0.2 select_reduce_fusion
  38.1 0.1 reduce_sum.92
  38.3 0.1 select_reduce_fusion.2
  38.5 225.3 %reduce-scatter.3.cloned.1.call-done = bf16[64,2048]{1,0:T(8,128)(2,1)} async-done(((bf16[2048,2048]{1,0:T(8,128)(2,1)}), bf16[64,2048]{1,0:T(8,128)(2,1)}) %reduce-scatter.3.cloned.1.call-update) | async-done | bytes 262160 | tf_op jit(solution)/shard_map/reduce_scatter | solution.py:70
  263.9 1.1 fusion.16
  265.0 1.2 convolution_convert_fusion.1
  266.2 2.0 broadcast_in_dim_reshape.3
  268.2 2.1 copy.84
  270.4 35.7 %all-gather.2.cloned.1.call-done = bf16[8,1,32,4,2048]{4,2,3,1,0:T(8,128)(2,1)} async-done(((bf16[1,1,32,4,2048]{4,2,3,1,0:T(8,128)(2,1)}), bf16[8,1,32,4,2048]{4,2,3,1,0:T(8,128)(2,1)}) %all-gather.2.cloned.1.call-update) | async-done | bytes 4194320 | tf_op jit(solution)/shard_map/all_gather | solution.py:120
  306.1 5.6 %copy.85 = bf16[8,1,32,4,2048]{4,3,0,1,2:T(4,128)(2,1)S(1)} copy(bf16[8,1,32,4,2048]{4,2,3,1,0:T(8,128)(2,1)} %all-gather.2.cloned.1.call-done) | data formatting | bytes 8388608 | tf_op jit(solution)/shard_map/all_gather | solution.py:120
  311.7 103.9 %all_to_all.10 = bf16[8,1,32,4,2048]{4,3,0,1,2:T(4,128)(2,1)S(1)} all-to-all(bf16[8,1,32,4,2048]{4,3,0,1,2:T(4,128)(2,1)S(1)} %copy.85), channel_id=1, replica_groups=mesh['expert'=8,'tensor'=32] {'tensor'}, dimensions={2} | all-to-all | bytes 8388608 | tf_op jit(solution)/shard_map/all_to_all | solution.py:121
  415.7 7.3 %fusion.7 = f32[8,1,32,4,2,704]{5,2,4,3,0,1:T(8,128)S(1)} fusion(bf16[1,2048,2,704]{1,3,2,0:T(8,128)(2,1)S(1)} %bitcast.83, bf16[8,1,32,4,2048]{4,3,0,1,2:T(4,128)(2,1)S(1)} %all_to_all.10), kind=kOutput, calls=%fused_computation.13 | convolution fusion | flops 5905580032 | bytes 15728640 | tf_op jit(solution)/shard_map/tsecd,sdgf->tsecgf/dot_general | solution.py:24
  422.9 1.0 fusion.5
  423.9 2.4 copy.87
  426.3 3.7 convert_element_type.95
  430.0 6.3 %convert_bitcast_fusion = bf16[1024,1,2048]{2,0,1:T(8,128)(2,1)} fusion(bf16[1024,704]{1,0:T(8,128)(2,1)} %convert_element_type.95, bf16[1,704,2048]{2,1,0:T(8,128)(2,1)S(1)} %copy-done), kind=kOutput, calls=%fused_computation.8 | convolution fusion | flops 2954887168 | bytes 8519680 | tf_op jit(solution)/shard_map/bsf,sfd->bsd/dot_general | solution.py:125
  436.5 0.1 reshape.190
  436.8 0.1 mul.206
  437.0 0.1 mul.205
  437.2 37.1 %reduce-scatter.5.cloned.1.call-done = bf16[128,1,2048]{2,0,1:T(8,128)(2,1)} async-done(((bf16[1024,1,2048]{2,0,1:T(8,128)(2,1)}), bf16[128,1,2048]{2,0,1:T(8,128)(2,1)}) %reduce-scatter.5.cloned.1.call-update) | async-done | bytes 524304 | tf_op jit(solution)/shard_map/reduce_scatter | solution.py:124
  474.3 2.0 reshape.179
  476.3 9.8 %all-to-all-start.1 = ((bf16[32,4,1,2048]{3,1,2,0:T(4,128)(2,1)}), bf16[32,4,1,2048]{3,1,2,0:T(4,128)(2,1)}, u32[]{:S(2)}, u32[]{:S(2)}) async-start(bf16[32,4,1,2048]{3,1,2,0:T(4,128)(2,1)} %bitcast.81), calls=%async_computation.3 | async-start | bytes 1048576 | tf_op jit(solution)/shard_map/all_to_all | solution.py:133
  486.1 0.2 fusion.23
  486.4 1.0 gather_fusion.1
  487.4 0.1 reshape.193
  487.7 15.7 %all-to-all-done.1 = bf16[32,4,1,2048]{3,1,2,0:T(4,128)(2,1)} async-done(((bf16[32,4,1,2048]{3,1,2,0:T(4,128)(2,1)}), bf16[32,4,1,2048]{3,1,2,0:T(4,128)(2,1)}, u32[]{:S(2)}, u32[]{:S(2)}) %all-to-all-start.1) | async-done | bytes 524320 | tf_op jit(solution)/shard_map/all_to_all | solution.py:133
  503.4 1.2 reshape.180
  504.5 1.7 gather_fusion
  506.3 1.4 gather.11
  507.6 0.3 fusion.22
  508.0 1.2 multiply_reduce_fusion
  509.3 0.8 multiply_convert_fusion
  (59 shorter events, 1.1 us)
Async XLA Ops:
  7.2 422.9 %copy-start = (bf16[1,704,2048]{2,1,0:T(8,128)(2,1)S(1)}, bf16[1,704,2048]{2,1,0:T(8,128)(2,1)}, u32[]{:S(2)}) copy-start(bf16[1,704,2048]{2,1,0:T(8,128)(2,1)} %param.26) | copy-start | bytes 8650756
  7.2 5.7 %copy-start.5 = (f32[2048,2]{0,1:T(2,128)S(1)}, f32[2048,2]{0,1:T(2,128)}, u32[]{:S(2)}) copy-start(f32[2048,2]{0,1:T(2,128)} %param.17) | copy-start | bytes 49156
  7.2 6.1 %copy-start.4 = (s32[2048,2]{0,1:T(2,128)S(1)}, s32[2048,2]{0,1:T(2,128)}, u32[]{:S(2)}) copy-start(s32[2048,2]{0,1:T(2,128)} %param.16) | copy-start | bytes 49156
  7.2 256.7 %reduce-scatter.3.cloned.1.call-start = ((), (), s32[]{:S(2)}) async-start(), calls=%async_computation.4 | async-start | bytes 8650752 | tf_op jit(solution)/shard_map/reduce_scatter | solution.py:70
  14.7 14.3 %copy-start.11 = (bf16[8,64,2048]{2,1,0:T(8,128)(2,1)S(1)}, bf16[8,64,2048]{2,1,0:T(8,128)(2,1)}, u32[]{:S(2)}) copy-start(bf16[8,64,2048]{2,1,0:T(8,128)(2,1)} %param.18) | copy-start | bytes 6291460
  35.9 0.7 copy-start.7
  35.9 0.7 copy-start.3
  35.9 0.8 copy-start.6
  36.0 1.0 copy-start.9
  36.0 2.4 copy-start.10
  36.0 227.9 %copy-start.2 = (bf16[64,2048]{1,0:T(8,128)(2,1)S(1)}, bf16[64,2048]{1,0:T(8,128)(2,1)}, u32[]{:S(2)}) copy-start(bf16[64,2048]{1,0:T(8,128)(2,1)} %param.14) | copy-start | bytes 786436
  36.0 270.1 %all-gather.2.cloned.1.call-start = ((), (), s32[]{:S(2)}) async-start(), calls=%async_computation.5 | async-start | bytes 4718592 | tf_op jit(solution)/shard_map/all_gather | solution.py:120
  265.0 221.1 %copy-start.1 = (bf16[64,2048]{1,0:T(8,128)(2,1)}, bf16[64,2048]{1,0:T(8,128)(2,1)S(1)}, u32[]{:S(2)}) copy-start(bf16[64,2048]{1,0:T(8,128)(2,1)S(1)} %get-tuple-element.9) | copy-start | bytes 786436
  270.4 203.9 %reduce-scatter.5.cloned.1.call-start = ((), (), s32[]{:S(2)}) async-start(), calls=%async_computation.6 | async-start | bytes 4718592 | tf_op jit(solution)/shard_map/reduce_scatter | solution.py:124
  306.1 109.5 %slice-start = ((s8[5767168]{0:T(1024)(128)(4,1)}), s8[4194304]{0:T(1024)(128)(4,1)S(1)}, s32[]{:S(2)}) async-start(s8[5767168]{0:T(1024)(128)(4,1)} %bitcast.82), calls=%async_computation.7 | async-start | bytes 8388608
  311.7 103.9 %slice-start.1 = ((s8[5767168]{0:T(1024)(128)(4,1)}), s8[1572864]{0:T(1024)(128)(4,1)S(1)}, s32[]{:S(2)}) async-start(s8[5767168]{0:T(1024)(128)(4,1)} %bitcast.82), calls=%async_computation.8 | async-start | bytes 3145728
  436.4 0.8 copy-start.8
  436.4 49.7 %copy-start.12 = (bf16[2048,8]{0,1:T(8,128)(2,1)S(1)}, bf16[2048,8]{0,1:T(8,128)(2,1)}, u32[]{:S(2)}) copy-start(bf16[2048,8]{0,1:T(8,128)(2,1)} %param.20) | copy-start | bytes 98308
  476.3 27.1 %all-to-all-start.1 = ((bf16[32,4,1,2048]{3,1,2,0:T(4,128)(2,1)}), bf16[32,4,1,2048]{3,1,2,0:T(4,128)(2,1)}, u32[]{:S(2)}, u32[]{:S(2)}) async-start(bf16[32,4,1,2048]{3,1,2,0:T(4,128)(2,1)} %bitcast.81), calls=%async_computation.3 | async-start | bytes 1048576 | tf_op jit(solution)/shard_map/all_to_all | solution.py:133
Sparse Core Ops, SparseCore 0:
  36.1 227.6 reduce-scatter.2
  270.5 35.6 all-gather.1
  436.5 37.7 reduce-scatter.4
where the time goes:
time: 517 us
  waiting for transfers between devices  314 us (61%)
  blocking collectives  104 us (20%)
  matrix products  36.2 us (7%)
  local copies, waits for them, and re-layouts  32.7 us (6%)
  between operations  14.1 us (3%)
  starting transfers between devices  9.88 us (2%)
  other arithmetic  5.94 us (1%)
    reduce_scatter x1, waiting for transfers between devices, per_device(): lax.psum_scatter(jnp.dot(row_block, weight_flat, preferred_element_type=j...  225 us
    all_to_all x1, blocking collectives, per_device(): lax.all_to_all(collected, 'tensor', split_axis=2, concat_axis=2, tiled=True)  104 us
    reduce_scatter x1, waiting for transfers between devices, per_device(): lax.psum_scatter(jnp.einsum('bsf,sfd->bsd', row_block, w_down, preferred_...  37.1 us
    all_gather x1, waiting for transfers between devices, per_device(): collected = lax.all_gather(send_rows[None], 'expert', axis=0, tiled=True)  35.7 us
    all_to_all x1, waiting for transfers between devices, per_device(): lax.all_to_all(results, 'tensor', split_axis=0, concat_axis=0, tiled=True)  15.7 us
    dot_general x1, matrix products, per_device(): jnp.einsum('tke,tck->tec', weighted, context_part).astype(jnp.bfloat16)  14.3 us
  transfers between devices with their start and end apart: 4, of which 4 were waited for; matrix products, arithmetic and copies ran while one was open for 1% of the time, Pallas kernels for 0%

commit v1 on v0

--- a/solution.py
+++ b/solution.py
@@ -117,7 +117,9 @@
     )
     send_rows = jnp.dot(placer, normed, preferred_element_type=jnp.float32).astype(jnp.bfloat16)
     send_rows = send_rows.reshape(slots, n_tensor, capacity_rows, model_width)
-    collected = lax.all_gather(send_rows[None], "expert", axis=0, tiled=True)
+    x = send_rows[None]
+    outgoing = jnp.stack([x] * lax.axis_size("expert"))
+    collected = jnp.concatenate(lax.all_to_all(outgoing, "expert", 0, 0), axis=0)
     arrived = lax.all_to_all(collected, "tensor", split_axis=2, concat_axis=2, tiled=True)
     hidden = activate(arrived, w_gate_up)
     row_block = hidden

time: 517 us -> 533 us (1.031)
  blocking collectives: 104 us -> 157 us
  waiting for transfers between devices: 314 us -> 278 us
    all_to_all x0 -> x1, blocking collectives: none -> 57.2 us  [per_device(): lax.all_to_all(outgoing, 'expert', 0, 0)]
    all_gather x1 -> x0, waiting for transfers between devices: 35.7 us -> none  [per_device(): collected = lax.all_gather(send_rows[None], 'expert', axis=0, tiled=True)]
    all_gather x1 -> x0, local copies, waits for them, and re-layouts: 5.57 us -> none  [per_device(): collected = lax.all_gather(send_rows[None], 'expert', axis=0, tiled=True)]
  transfers between devices with their start and end apart: 4 -> 3, of which waited for: 4 -> 3; matrix products, arithmetic and copies ran while one was open for 1% -> 1% of each run, Pallas kernels for 0% -> 0%
where the time goes in v1:
time: 533 us; the launch traced here: 532 us
  waiting for transfers between devices  278 us (52%)
  blocking collectives  157 us (29%)
  matrix products  36.3 us (7%)
  local copies, waits for them, and re-layouts  30.2 us (6%)
  between operations  14.4 us (3%)
  starting transfers between devices  9.82 us (2%)
  other arithmetic  6.73 us (1%)
    reduce_scatter x1, waiting for transfers between devices, per_device(): lax.psum_scatter(jnp.dot(row_block, weight_flat, preferred_element_type=j...  225 us
    all_to_all x1, blocking collectives, per_device(): lax.all_to_all(collected, 'tensor', split_axis=2, concat_axis=2, tiled=True)  99.9 us
    all_to_all x1, blocking collectives, per_device(): lax.all_to_all(outgoing, 'expert', 0, 0)  57.2 us
    reduce_scatter x1, waiting for transfers between devices, per_device(): lax.psum_scatter(jnp.einsum('bsf,sfd->bsd', row_block, w_down, preferred_...  37.6 us
    all_to_all x1, waiting for transfers between devices, per_device(): lax.all_to_all(results, 'tensor', split_axis=0, concat_axis=0, tiled=True)  15.7 us
    dot_general x1, matrix products, per_device(): jnp.einsum('tke,tck->tec', weighted, context_part).astype(jnp.bfloat16)  14.3 us
  transfers between devices with their start and end apart: 3, of which 3 were waited for; matrix products, arithmetic and copies ran while one was open for 1% of the time, Pallas kernels for 0%

profile of v1, /device:TPU:7, one launch (start us, length us, event | category | flops | bytes accessed | tf_op | source)
XLA Modules:
  0.0 532.3 jit_solution(17688067235365034659)
XLA Ops:
  7.2 2.2 copy.77
  9.4 1.4 reshape.182
  10.8 2.1 copy.78
  12.9 0.8 broadcast_subtract_fusion
  13.8 0.3 copy.76
  14.1 1.4 copy.75
  15.5 14.3 %convolution_convert_fusion = bf16[2048,8,64]{2,1,0:T(8,128)(2,1)S(1)} fusion(bf16[2048,64,2]{1,2,0:T(2,128)(2,1)} %copy.78, bf16[2048,2]{1,0:T(8,128)(2,1)S(1)} %copy.76, s32[2048,2]{1,0:T(8,128)} %copy.75), kind=kOutput, calls=%fused_computation.14 | convolution fusion | flops 4259840 | bytes 2646016 | tf_op jit(solution)/shard_map/tke,tck->tec/dot_general | solution.py:64
  29.8 7.0 %bitcast_convert_fusion = bf16[2048,2048]{1,0:T(8,128)(2,1)} fusion(bf16[8,64,2048]{2,1,0:T(8,128)(2,1)S(1)} %copy-done.10, bf16[2048,8,64]{2,1,0:T(8,128)(2,1)S(1)} %convolution_convert_fusion), kind=kOutput, calls=%fused_computation.2 | convolution fusion | flops 4299161600 | bytes 12582912 | tf_op jit(solution)/shard_map/dot_general | solution.py:71
  36.9 0.6 copy-done.6
  37.5 0.1 convert_reduce_fusion.1
  37.7 0.1 and_select_fusion.1
  38.0 0.1 eq.133
  38.1 0.1 eq.119
  38.3 0.2 convert_reduce_fusion
  38.6 0.2 reduce_window_sum.11
  38.7 0.2 select_reduce_fusion
  38.9 0.1 reduce_sum.92
  39.1 0.1 select_reduce_fusion.2
  39.3 224.6 %reduce-scatter.3.cloned.1.call-done = bf16[64,2048]{1,0:T(8,128)(2,1)} async-done(((bf16[2048,2048]{1,0:T(8,128)(2,1)}), bf16[64,2048]{1,0:T(8,128)(2,1)}) %reduce-scatter.3.cloned.1.call-update) | async-done | bytes 262160 | tf_op jit(solution)/shard_map/reduce_scatter | solution.py:70
  264.0 1.1 fusion.16
  265.1 1.1 convolution_convert_fusion.1
  266.3 2.0 stack_broadcast_in_dim_reshape.2
  268.3 1.3 copy.84
  269.7 0.5 stack.12
  270.2 57.2 %all_to_all.15 = bf16[8,1,1,32,4,2048]{5,3,4,2,1,0:T(8,128)(2,1)S(1)} all-to-all(bf16[8,1,1,32,4,2048]{5,3,4,2,1,0:T(8,128)(2,1)S(1)} %stack.12), channel_id=1, replica_groups=mesh['expert'=8,'tensor'=32] {'expert'}, dimensions={0} | all-to-all | bytes 8388608 | tf_op jit(solution)/shard_map/all_to_all | solution.py:122
  327.4 3.2 copy.85
  330.6 99.9 %all_to_all.16 = bf16[8,1,32,4,2048]{4,3,0,1,2:T(4,128)(2,1)S(1)} all-to-all(bf16[8,1,32,4,2048]{4,3,0,1,2:T(4,128)(2,1)S(1)} %copy.85), channel_id=1, replica_groups=mesh['expert'=8,'tensor'=32] {'tensor'}, dimensions={2} | all-to-all | bytes 8388608 | tf_op jit(solution)/shard_map/all_to_all | solution.py:123
  430.5 7.3 %fusion.7 = f32[8,1,32,4,2,704]{5,2,4,3,0,1:T(8,128)S(1)} fusion(bf16[1,2048,2,704]{1,3,2,0:T(8,128)(2,1)S(1)} %bitcast.85, bf16[8,1,32,4,2048]{4,3,0,1,2:T(4,128)(2,1)S(1)} %all_to_all.16), kind=kOutput, calls=%fused_computation.13 | convolution fusion | flops 5905580032 | bytes 15728640 | tf_op jit(solution)/shard_map/tsecd,sdgf->tsecgf/dot_general | solution.py:24
  437.8 1.0 fusion.5
  438.8 2.4 copy.87
  441.2 3.7 convert_element_type.95
  444.9 6.4 %convert_bitcast_fusion = bf16[1024,1,2048]{2,0,1:T(8,128)(2,1)} fusion(bf16[1024,704]{1,0:T(8,128)(2,1)} %convert_element_type.95, bf16[1,704,2048]{2,1,0:T(8,128)(2,1)S(1)} %copy-done), kind=kOutput, calls=%fused_computation.8 | convolution fusion | flops 2954887168 | bytes 8519680 | tf_op jit(solution)/shard_map/bsf,sfd->bsd/dot_general | solution.py:127
  451.4 0.1 reshape.198
  451.6 0.1 mul.206
  451.9 0.1 mul.205
  452.1 37.6 %reduce-scatter.5.cloned.1.call-done = bf16[128,1,2048]{2,0,1:T(8,128)(2,1)} async-done(((bf16[1024,1,2048]{2,0,1:T(8,128)(2,1)}), bf16[128,1,2048]{2,0,1:T(8,128)(2,1)}) %reduce-scatter.5.cloned.1.call-update) | async-done | bytes 524304 | tf_op jit(solution)/shard_map/reduce_scatter | solution.py:126
  489.7 2.0 reshape.187
  491.7 9.7 %all-to-all-start.2 = ((bf16[32,4,1,2048]{3,1,2,0:T(4,128)(2,1)}), bf16[32,4,1,2048]{3,1,2,0:T(4,128)(2,1)}, u32[]{:S(2)}, u32[]{:S(2)}) async-start(bf16[32,4,1,2048]{3,1,2,0:T(4,128)(2,1)} %bitcast.83), calls=%async_computation.4 | async-start | bytes 1048576 | tf_op jit(solution)/shard_map/all_to_all | solution.py:135
  501.5 0.2 fusion.23
  501.7 1.0 gather_fusion.1
  502.8 0.1 reshape.201
  503.0 15.7 %all-to-all-done.2 = bf16[32,4,1,2048]{3,1,2,0:T(4,128)(2,1)} async-done(((bf16[32,4,1,2048]{3,1,2,0:T(4,128)(2,1)}), bf16[32,4,1,2048]{3,1,2,0:T(4,128)(2,1)}, u32[]{:S(2)}, u32[]{:S(2)}) %all-to-all-start.2) | async-done | bytes 524320 | tf_op jit(solution)/shard_map/all_to_all | solution.py:135
  518.8 1.2 reshape.188
  519.9 1.7 gather_fusion
  521.7 1.4 gather.11
  523.0 0.3 fusion.22
  523.4 1.2 multiply_reduce_fusion
  524.7 0.8 multiply_convert_fusion
  (56 shorter events, 1.2 us)
Async XLA Ops:
  7.2 437.7 %copy-start = (bf16[1,704,2048]{2,1,0:T(8,128)(2,1)S(1)}, bf16[1,704,2048]{2,1,0:T(8,128)(2,1)}, u32[]{:S(2)}) copy-start(bf16[1,704,2048]{2,1,0:T(8,128)(2,1)} %param.26) | copy-start | bytes 8650756
  7.2 6.9 %copy-start.4 = (s32[2048,2]{0,1:T(2,128)S(1)}, s32[2048,2]{0,1:T(2,128)}, u32[]{:S(2)}) copy-start(s32[2048,2]{0,1:T(2,128)} %param.16) | copy-start | bytes 49156
  7.2 256.8 %reduce-scatter.3.cloned.1.call-start = ((), (), s32[]{:S(2)}) async-start(), calls=%async_computation.5 | async-start | bytes 8650752 | tf_op jit(solution)/shard_map/reduce_scatter | solution.py:70
  15.5 14.3 %copy-start.10 = (bf16[8,64,2048]{2,1,0:T(8,128)(2,1)S(1)}, bf16[8,64,2048]{2,1,0:T(8,128)(2,1)}, u32[]{:S(2)}) copy-start(bf16[8,64,2048]{2,1,0:T(8,128)(2,1)} %param.18) | copy-start | bytes 6291460
  36.7 0.7 copy-start.6
  36.8 0.7 copy-start.3
  36.8 0.8 copy-start.5
  36.8 1.0 copy-start.8
  36.8 2.4 copy-start.9
  36.8 227.2 %copy-start.2 = (bf16[64,2048]{1,0:T(8,128)(2,1)S(1)}, bf16[64,2048]{1,0:T(8,128)(2,1)}, u32[]{:S(2)}) copy-start(bf16[64,2048]{1,0:T(8,128)(2,1)} %param.14) | copy-start | bytes 786436
  36.8 452.9 %reduce-scatter.5.cloned.1.call-start = ((), (), s32[]{:S(2)}) async-start(), calls=%async_computation.6 | async-start | bytes 4718592 | tf_op jit(solution)/shard_map/reduce_scatter | solution.py:126
  265.1 236.4 %copy-start.1 = (bf16[64,2048]{1,0:T(8,128)(2,1)}, bf16[64,2048]{1,0:T(8,128)(2,1)S(1)}, u32[]{:S(2)}) copy-start(bf16[64,2048]{1,0:T(8,128)(2,1)S(1)} %get-tuple-element.9) | copy-start | bytes 786436
  327.4 103.1 %slice-start = ((s8[5767168]{0:T(1024)(128)(4,1)}), s8[4194304]{0:T(1024)(128)(4,1)S(1)}, s32[]{:S(2)}) async-start(s8[5767168]{0:T(1024)(128)(4,1)} %bitcast.84), calls=%async_computation.7 | async-start | bytes 8388608
  330.6 99.9 %slice-start.1 = ((s8[5767168]{0:T(1024)(128)(4,1)}), s8[1572864]{0:T(1024)(128)(4,1)S(1)}, s32[]{:S(2)}) async-start(s8[5767168]{0:T(1024)(128)(4,1)} %bitcast.84), calls=%async_computation.8 | async-start | bytes 3145728
  451.3 0.8 copy-start.7
  451.3 50.2 %copy-start.11 = (bf16[2048,8]{0,1:T(8,128)(2,1)S(1)}, bf16[2048,8]{0,1:T(8,128)(2,1)}, u32[]{:S(2)}) copy-start(bf16[2048,8]{0,1:T(8,128)(2,1)} %param.20) | copy-start | bytes 98308
  491.7 27.1 %all-to-all-start.2 = ((bf16[32,4,1,2048]{3,1,2,0:T(4,128)(2,1)}), bf16[32,4,1,2048]{3,1,2,0:T(4,128)(2,1)}, u32[]{:S(2)}, u32[]{:S(2)}) async-start(bf16[32,4,1,2048]{3,1,2,0:T(4,128)(2,1)} %bitcast.83), calls=%async_computation.4 | async-start | bytes 1048576 | tf_op jit(solution)/shard_map/all_to_all | solution.py:135
Sparse Core Ops, SparseCore 0:
  36.9 226.9 reduce-scatter.2
  451.4 38.2 reduce-scatter.4
